TPU v7x, 32 devices: a whole 2x2x4 slice. The times are simulated.
32 devices in a mesh: groups: 2 (over x), ctx: 4 (over y, core), head: 4 (over z).
Axes of the slice: x: 2, y: 2, z: 4, core: 2. Of those that a mesh axis runs over, the one named last changes fastest.
Arguments:
- tokens: bfloat16 [8192, 2048], P(('groups', 'ctx')), parts along dimension 0, may hold values from -30 to 30
- norm_one: float32 [2048], replicated, may hold values from 0.1 to 1.9
- w_qkv1: bfloat16 [2048, 3, 2048], P(None, None, 'head'), may hold values from -0.125 to 0.125
- lin_gain: float32 [2048], P('head'), may hold values from 0.1 to 1.9
- w_out1: bfloat16 [2048, 2048], P('head'), may hold values from -0.125 to 0.125
- norm_two: float32 [2048], replicated, may hold values from 0.1 to 1.9
- w_qkv2: bfloat16 [2048, 3, 2048], P(None, None, 'head'), may hold values from -0.125 to 0.125
- q_gain: float32 [128], replicated, may hold values from 0.4 to 2.5
- k_gain: float32 [128], replicated, may hold values from 0.4 to 2.5
- w_out2: bfloat16 [2048, 2048], P('head'), may hold values from -0.125 to 0.125
- neighbours: int32 [16, 8], P('ctx'), may hold values from -1 to 15, as said below
Outputs:
- mixed: bfloat16 [8192, 2048], P(('groups', 'ctx', 'head')), parts along dimension 0
There are 2 independent parts, one for each index of `groups`. A program takes and returns all parts, laid end to end along the dimension named above; an argument that names none is the same for every part. Nothing has to cross between parts.
Inputs may be any that keep to these rules, and one draw needn't show every extreme that they name: `neighbours`: tile (i, j, l) of the 4 x 2 x 2 grid is number (i * 2 + j) * 2 + l, and its tokens are a whole tile of the stream. Entry 0 of row t is t itself; every other entry is -1 or a tile other than t whose grid position differs from t's by at most one in each dimension; the tiles of one row are distinct.
All inputs are finite; a program needn't handle non-finite values.
Results may differ from a plain program's by a relative error of at most 0.013.
Values may be sent and summed in bfloat16 or wider, within the bound.
No kernel may reach another device: no remote copies, remote signals or barrier semaphores. Data moves between devices by JAX's collectives and lax.ppermute only.
A program may use at most 192 MiB of HBM per device.

v0:
```python
import math
import jax
import jax.numpy as jnp
from jax import lax
from jax.sharding import PartitionSpec as P

TILE = 256
GY = 2
GZ = 2
EPS = 1e-06


def with_halo(shard, sides, width):
    for axis, dim in sides:
        size, length = (lax.axis_size(axis), shard.shape[dim])
        up = [(i, (i + 1) % size) for i in range(size - 1)]
        down = [(j, i) for i, j in up]
        last = lax.slice_in_dim(shard, length - width, length, axis=dim)
        first = lax.slice_in_dim(shard, 0, width, axis=dim)
        before = lax.ppermute(last, axis, up)
        after = lax.ppermute(first, axis, down)
        shard = jnp.concatenate([before, shard, after], axis=dim)
    return shard


def rms_rows(value, gain):
    mean_sq = jnp.mean(value * value, axis=-1, keepdims=True)
    return value * lax.rsqrt(mean_sq + EPS) * gain


def feature_map(value):
    return jnp.where(value > 0, value + 1.0, jnp.exp(jnp.minimum(value, 0.0)))


def split_two(value):
    high_part = value.astype(jnp.bfloat16)
    low_part = (value - high_part.astype(jnp.float32)).astype(jnp.bfloat16)
    return (high_part, low_part)


def on_device(
    tokens, norm_one, w_qkv1, lin_gain, w_out1, norm_two, w_qkv2, q_gain, k_gain, w_out2, neighbours
):
    f32, bf16 = (jnp.float32, jnp.bfloat16)
    tok_rows, feature_width = tokens.shape
    inner_dev = w_qkv1.shape[2]
    head_dim = q_gain.shape[0]
    heads_dev = inner_dev // head_dim
    block_rows = 2 * TILE
    block_count = tok_rows // block_rows
    rows_mine = tok_rows // lax.axis_size("head")
    head_index = lax.axis_index("head")
    ctx_index = lax.axis_index("ctx")
    ctx_size = lax.axis_size("ctx")
    normed = rms_rows(tokens.astype(f32), norm_one).astype(bf16)
    projected = jnp.dot(
        normed, w_qkv1.reshape(feature_width, 3 * inner_dev), preferred_element_type=f32
    )
    projected = projected.reshape(tok_rows, 3, heads_dev, head_dim)
    query_map = feature_map(projected[:, 0]).astype(bf16)
    key_map = feature_map(projected[:, 1]).astype(bf16)
    value_one = projected[:, 2].astype(bf16)
    q_blocks = query_map.reshape(block_count, block_rows, heads_dev, head_dim)
    k_blocks = key_map.reshape(block_count, block_rows, heads_dev, head_dim)
    v_blocks = value_one.reshape(block_count, block_rows, heads_dev, head_dim)
    block_states = jnp.einsum("nthe,nthf->nhef", k_blocks, v_blocks, preferred_element_type=f32)
    own_total = jnp.sum(block_states, axis=0)
    all_totals = lax.all_gather(own_total.astype(bf16), "ctx", axis=0).astype(f32)
    earlier_dev = jnp.arange(ctx_size, dtype=jnp.int32) < ctx_index
    carried = jnp.sum(jnp.where(earlier_dev[:, None, None, None], all_totals, 0.0), axis=0)
    causal = lax.broadcasted_iota(jnp.int32, (block_rows, block_rows), 0) >= lax.broadcasted_iota(
        jnp.int32, (block_rows, block_rows), 1
    )
    w_qkv2_flat = w_qkv2.reshape(feature_width, 3 * inner_dev)
    residual_parts = []
    q_parts, k_parts, v_parts = ([], [], [])
    previous = None
    for n in range(block_count):
        q_n, k_n, v_n = (q_blocks[n], k_blocks[n], v_blocks[n])
        scores = jnp.einsum("the,she->hts", q_n, k_n, preferred_element_type=f32)
        scores = jnp.where(causal, scores, 0.0)
        score_high, score_low = split_two(scores)
        within = jnp.einsum("hts,she->the", score_high, v_n, preferred_element_type=f32)
        within = within + jnp.einsum("hts,she->the", score_low, v_n, preferred_element_type=f32)
        state_high, state_low = split_two(carried)
        carried_term = jnp.einsum("the,hef->thf", q_n, state_high, preferred_element_type=f32)
        carried_term = carried_term + jnp.einsum(
            "the,hef->thf", q_n, state_low, preferred_element_type=f32
        )
        carried = carried + block_states[n]
        combined = within + carried_term
        attn_n = (
            rms_rows(combined, lin_gain.reshape(heads_dev, head_dim))
            .astype(bf16)
            .reshape(block_rows, inner_dev)
        )
        partial = jnp.dot(attn_n, w_out1, preferred_element_type=f32).astype(bf16)
        if previous is not None:
            partial, previous = lax.optimization_barrier((partial, previous))
            residual_parts[-1] = previous
        summed = lax.psum(partial, "head").astype(f32)
        tokens_n = tokens[n * block_rows : (n + 1) * block_rows].astype(f32)
        residual_n = (tokens_n + summed).astype(bf16)
        residual_parts.append(residual_n)
        previous = residual_n
        normed_n = rms_rows(residual_n.astype(f32), norm_two).astype(bf16)
        proj_n = jnp.dot(normed_n, w_qkv2_flat, preferred_element_type=f32)
        proj_n = proj_n.reshape(block_rows, 3, heads_dev, head_dim)
        q_parts.append(rms_rows(proj_n[:, 0], q_gain).astype(bf16))
        k_parts.append(rms_rows(proj_n[:, 1], k_gain).astype(bf16))
        v_parts.append(proj_n[:, 2].astype(bf16))
    residual = jnp.concatenate(residual_parts, axis=0)
    query_hat = jnp.concatenate(q_parts, axis=0)
    key_hat = jnp.concatenate(k_parts, axis=0)
    value_two = jnp.concatenate(v_parts, axis=0)
    key_value = jnp.stack([key_hat, value_two], axis=1).reshape(tok_rows, 2 * inner_dev)
    plane_tiles = GY * GZ
    widened = with_halo(key_value, (("ctx", 0),), plane_tiles * TILE)
    buffer_rows = widened.shape[0]
    buffer_tiles = buffer_rows // TILE
    tile_count = tok_rows // TILE
    base_tile = ctx_index * tile_count - plane_tiles
    widened = widened.reshape(buffer_rows, 2, heads_dev, head_dim)
    buffer_ids = base_tile + jnp.arange(buffer_tiles, dtype=jnp.int32)
    valid = jnp.any(
        (neighbours[:, :, None] == buffer_ids[None, None, :]) & (neighbours[:, :, None] >= 0),
        axis=1,
    )
    valid_keys = jnp.repeat(valid, TILE, axis=1)
    query_tiles = query_hat.reshape(tile_count, TILE, heads_dev, head_dim)
    score_scale = 1.0 / math.sqrt(head_dim)
    tile_scores = (
        jnp.einsum("pthe,she->phts", query_tiles, widened[:, 0], preferred_element_type=f32)
        * score_scale
    )
    unnormed = jnp.where(valid_keys[:, None, None, :], jnp.exp(tile_scores), 0.0)
    weights = (unnormed / jnp.sum(unnormed, axis=-1, keepdims=True)).astype(bf16)
    attn_two = jnp.einsum("phts,she->pthe", weights, widened[:, 1], preferred_element_type=f32)
    attn_two = attn_two.astype(bf16).reshape(tok_rows, inner_dev)
    summed_two = lax.psum_scatter(
        jnp.dot(attn_two, w_out2, preferred_element_type=f32).astype(bf16),
        "head",
        scatter_dimension=0,
        tiled=True,
    ).astype(f32)
    residual_mine = lax.dynamic_slice_in_dim(residual, head_index * rows_mine, rows_mine, 0)
    return (residual_mine.astype(f32) + summed_two).astype(bf16)


def solution(mesh):
    in_specs = (
        P(("groups", "ctx"), None),
        P(),
        P(None, None, "head"),
        P("head"),
        P("head", None),
        P(),
        P(None, None, "head"),
        P(),
        P(),
        P("head", None),
        P("ctx", None),
    )
    out_specs = P(("groups", "ctx", "head"), None)
    return jax.shard_map(
        on_device, mesh=mesh, in_specs=in_specs, out_specs=out_specs, check_vma=False
    )
```

profile of v0, /device:TPU:0, one launch (start us, length us, event | category | flops | bytes accessed | tf_op | source)
XLA Modules:
  0.0 424.5 jit_solution(1946575152552089847)
XLA Ops:
  6.5 0.1 iota_compare_fusion
  6.6 3.2 fusion.2
  9.8 0.0 copy-start.15
  9.9 8.8 %copy.60 = bf16[2048,3,512]{0,2,1:T(8,128)(2,1)} copy(bf16[2048,3,512]{2,0,1:T(8,128)(2,1)} %param.13) | data formatting | bytes 12582912 | tf_op args[2]
  18.7 10.3 %fusion.12 = f32[1024,3,4,128]{3,0,2,1:T(8,128)S(1)} fusion(bf16[3,4,128,2048]{3,2,1,0:T(8,128)(2,1)} %bitcast.165, bf16[1024,2048]{1,0:T(8,128)(2,1)} %param.11, f32[2048]{0:T(1024)S(1)} %copy-done.15, f32[1024]{0:T(1024)S(1)} %add_rsqrt_fusion.6), kind=kOutput, calls=%fused_computation.21 | convolution fusion | flops 6450839552 | bytes 16789504 | tf_op jit(solution)/shard_map/dot_general | solution.py:56
  29.0 1.1 slice.199
  30.1 1.0 select_convert_fusion.4
  31.1 2.6 fusion.56
  33.7 2.7 fusion.57
  36.4 2.0 fusion.73
  38.5 8.8 %all-gather = bf16[16,128,128]{2,1,0:T(8,128)(2,1)S(1)} all-gather(bf16[4,128,128]{2,1,0:T(8,128)(2,1)S(1)} %get-tuple-element.27), channel_id=2, replica_groups=mesh['groups'=2,'ctx'=4,'head'=4] {'ctx'}, dimensions={0}, use_global_device_ids=true | all-gather | bytes 655360 | tf_op jit(solution)/shard_map/all_gather | solution.py:68
  47.3 0.2 fusion.50
  47.5 0.3 fusion.59
  47.8 0.3 convolution_add_fusion
  48.2 0.4 fusion.58
  48.6 0.4 convolution_add_fusion.1
  48.9 1.1 copy-done.3
  50.0 0.3 copy-done.4
  50.3 0.9 fusion.18
  51.2 0.6 copy-done.2
  51.8 0.9 fusion.17
  52.7 1.1 multiply_reduce_fusion.4
  53.8 0.0 copy-start.12
  53.8 1.1 multiply_reduce_fusion.5
  54.9 0.3 multiply_convert_fusion.4
  55.2 2.6 convolution_convert_fusion.1
  57.7 0.0 all-reduce.3.cloned.1.call-update
  57.8 0.0 all-reduce.5.cloned.1.call-start
  57.8 2.6 convolution_convert_fusion.2
  60.4 84.9 %all-reduce.3.cloned.1.call-done = bf16[512,2048]{1,0:T(8,128)(2,1)} async-done(((bf16[512,2048]{1,0:T(8,128)(2,1)}), bf16[512,2048]{1,0:T(8,128)(2,1)}) %all-reduce.3.cloned.1.call-update) | async-done | bytes 2097168 | tf_op jit(solution)/shard_map/psum | solution.py:101
  145.3 3.2 fusion.5
  148.5 0.0 all-reduce.5.cloned.1.call-update
  148.5 0.3 reduce-scatter.2.cloned.1.call-start
  148.8 9.3 %copy.71 = bf16[2048,3,512]{0,2,1:T(8,128)(2,1)} copy(bf16[2048,3,512]{2,0,1:T(8,128)(2,1)} %param.17) | data formatting | bytes 12582912 | tf_op args[6]
  158.1 5.7 %fusion.25 = f32[512,3,4,128]{3,0,2,1:T(8,128)S(1)} fusion(bf16[3,4,128,2048]{3,2,1,0:T(8,128)(2,1)} %bitcast.163, bf16[512,2048]{1,0:T(8,128)(2,1)S(1)} %get-tuple-element.7, f32[2048]{0:T(1024)S(1)} %copy-done.16, f32[512]{0:T(512)S(1)} %add_rsqrt_fusion.8), kind=kOutput, calls=%fused_computation.45 | convolution fusion | flops 3225419776 | bytes 11544576 | tf_op jit(solution)/shard_map/dot_general | solution.py:107
  163.9 0.6 multiply_reduce_fusion.3
  164.5 1.0 copy-done.7
  165.6 0.1 fusion.54
  165.6 68.5 %all-reduce.5.cloned.1.call-done = bf16[512,2048]{1,0:T(8,128)(2,1)} async-done(((bf16[512,2048]{1,0:T(8,128)(2,1)}), bf16[512,2048]{1,0:T(8,128)(2,1)}) %all-reduce.5.cloned.1.call-update) | async-done | bytes 2097168 | tf_op jit(solution)/shard_map/psum | solution.py:101
  234.1 3.2 fusion.8
  237.4 6.5 %fusion.22 = f32[512,3,4,128]{3,0,2,1:T(8,128)S(1)} fusion(bf16[3,4,128,2048]{3,2,1,0:T(8,128)(2,1)} %bitcast.164, bf16[512,2048]{1,0:T(8,128)(2,1)S(1)} %get-tuple-element.16, f32[512]{0:T(512)S(1)} %add_rsqrt_fusion.7, f32[2048]{0:T(1024)S(1)} %copy-done.16), kind=kOutput, calls=%fused_computation.43 | convolution fusion | flops 3225419776 | bytes 11544576 | tf_op jit(solution)/shard_map/dot_general | solution.py:107
  243.9 0.6 multiply_reduce_fusion.2
  244.5 0.1 fusion.55
  244.6 0.1 maximum_bitcast_fusion.1
  244.7 1.0 copy-done.8
  245.8 1.4 multiply_convert_fusion.2
  247.2 0.1 maximum_bitcast_fusion
  247.3 1.5 pad_maximum_fusion.1
  248.7 4.0 copy.72
  252.7 1.3 collective-permute-start.1
  254.0 4.4 %collective-permute-start = (bf16[1024,1024]{0,1:T(8,128)(2,1)}, bf16[1024,1024]{0,1:T(8,128)(2,1)}, u32[]{:S(2)}, u32[]{:S(2)}) collective-permute-start(bf16[1024,1024]{0,1:T(8,128)(2,1)} %bitcast.169), channel_id=1, source_target_pairs={{0,4},{4,8},{8,12},{1,5},{5,9},{9,13},{2,6},{6,10},{10,14},{3,7},{... | collective-permute-start | bytes 6291464 | tf_op jit(solution)/shard_map/ppermute | solution.py:20
  258.4 0.1 and_reduce_fusion
  258.5 0.1 broadcast_bitcast_fusion
  258.6 1.0 pad_maximum_fusion.2
  259.6 3.9 copy.74
  263.6 4.0 copy.73
  267.5 3.1 pad_maximum_fusion
  270.7 19.7 %fusion = (f32[4,4,256]{2,0,1:T(4,128)S(1)}, f32[4,3072,4,256]{3,1,2,0:T(8,128)}) fusion(pred[4,3072]{1,0:T(4,128)(4,1)S(1)} %bitcast.174, bf16[4,256,4,128]{3,1,0,2:T(8,128)(2,1)S(1)} %bitcast.170, bf16[3072,2,4,128]{3,0,2,1:T(8,128)(2,1)S(1)} %pad_maximum_fusion), kind=kOutput, calls=%fused_computation.2 | convolution fusion | flops 3258970112 | bytes 54554624 | tf_op jit(solution)/shard_map/pthe,she->phts/dot_general | solution.py:133
  290.3 22.4 %fusion.40 = bf16[4,256,4,128]{1,3,0,2:T(8,128)(2,1)S(1)} fusion(f32[4,3072,4,256]{3,1,2,0:T(8,128)} %get-tuple-element.34, f32[4,4,256]{2,0,1:T(4,128)S(1)} %get-tuple-element.33, pred[4,3072]{1,0:T(4,128)(4,1)S(1)} %bitcast.175, bf16[3072,2,4,128]{3,0,2,1:T(8,128)(2,1)S(1)} %pad_maximum_fusion), kind=kOutput, calls=%fused_computation.64 | convolution fusion | flops 3272081408 | bytes 54554624 | tf_op jit(solution)/shard_map/phts,she->pthe/dot_general | solution.py:138
  312.7 0.7 copy.77
  313.4 5.9 %convolution_convert_fusion = bf16[1024,2048]{1,0:T(8,128)(2,1)} fusion(bf16[512,2048]{1,0:T(8,128)(2,1)} %param.20, bf16[128,8,4,128]{3,2,1,0:T(4,128)(2,1)S(1)} %bitcast.171), kind=kOutput, calls=%fused_computation.32 | convolution fusion | flops 2149580800 | bytes 7340032 | tf_op jit(solution)/shard_map/dot_general | solution.py:141
  319.3 0.0 reduce-scatter.2.cloned.1.call-update
  319.3 95.4 %reduce-scatter.2.cloned.1.call-done = bf16[256,2048]{1,0:T(8,128)(2,1)} async-done(((bf16[1024,2048]{1,0:T(8,128)(2,1)}), bf16[256,2048]{1,0:T(8,128)(2,1)}) %reduce-scatter.2.cloned.1.call-update) | async-done | bytes 1048592 | tf_op jit(solution)/shard_map/reduce_scatter | solution.py:140
  414.7 3.3 add_convert_fusion.2
  (42 shorter events, 0.2 us)
Async XLA Ops:
  6.5 48.6 %copy-start = (bf16[512,2048]{1,0:T(8,128)(2,1)S(1)}, bf16[512,2048]{1,0:T(8,128)(2,1)}, u32[]{:S(2)}) copy-start(bf16[512,2048]{1,0:T(8,128)(2,1)} %param.15) | copy-start | bytes 6291460
  6.5 138.7 %all-reduce.3.cloned.1.call-start = ((), (), s32[]{:S(2)}) async-start(), calls=%async_computation.1 | async-start | bytes 4194304 | tf_op jit(solution)/shard_map/psum | solution.py:101
  9.8 8.9 %copy-start.15 = (f32[2048]{0:T(1024)S(1)}, f32[2048]{0:T(1024)}, u32[]{:S(2)}) copy-start(f32[2048]{0:T(1024)} %param.12) | copy-start | bytes 24580
  31.1 2.7 copy-start.9
  47.8 2.2 copy-start.3
  47.8 2.5 copy-start.4
  48.5 3.2 copy-start.2
  53.8 1.1 copy-start.12
  57.8 176.4 %all-reduce.5.cloned.1.call-start = ((), (), s32[]{:S(2)}) async-start(), calls=%async_computation.2 | async-start | bytes 4194304 | tf_op jit(solution)/shard_map/psum | solution.py:101
  148.5 9.6 %copy-start.5 = (bf16[512,2048]{1,0:T(8,128)(2,1)}, bf16[512,2048]{1,0:T(8,128)(2,1)S(1)}, u32[]{:S(2)}) copy-start(bf16[512,2048]{1,0:T(8,128)(2,1)S(1)} %get-tuple-element.7) | copy-start | bytes 6291460
  148.5 9.6 %copy-start.16 = (f32[2048]{0:T(1024)S(1)}, f32[2048]{0:T(1024)}, u32[]{:S(2)}) copy-start(f32[2048]{0:T(1024)} %param.16) | copy-start | bytes 24580
  148.5 266.2 %reduce-scatter.2.cloned.1.call-start = ((), (), s32[]{:S(2)}) async-start(), calls=%async_computation.3 | async-start | bytes 5242880 | tf_op jit(solution)/shard_map/reduce_scatter | solution.py:140
  163.9 1.7 copy-start.7
  237.3 6.5 %copy-start.6 = (bf16[512,2048]{1,0:T(8,128)(2,1)}, bf16[512,2048]{1,0:T(8,128)(2,1)S(1)}, u32[]{:S(2)}) copy-start(bf16[512,2048]{1,0:T(8,128)(2,1)S(1)} %get-tuple-element.16) | copy-start | bytes 6291460
  243.9 1.9 copy-start.8
  243.9 1.9 copy-start.13
  243.9 1.9 copy-start.14
  247.2 11.1 %copy-start.11 = (s32[4,8]{1,0:T(4,128)S(1)}, s32[4,8]{1,0:T(4,128)}, u32[]{:S(2)}) copy-start(s32[4,8]{1,0:T(4,128)} %param.21) | copy-start | bytes 388
  252.7 6.9 %collective-permute-start.1 = (bf16[1024,1024]{0,1:T(8,128)(2,1)}, bf16[1024,1024]{0,1:T(8,128)(2,1)}, u32[]{:S(2)}, u32[]{:S(2)}) collective-permute-start(bf16[1024,1024]{0,1:T(8,128)(2,1)} %bitcast.168), channel_id=1, source_target_pairs={{4,0},{8,4},{12,8},{5,1},{9,5},{13,9},{6,2},{10,6},{14,10},{7,3},{... | collective-permute-start | bytes 6291464 | tf_op jit(solution)/shard_map/ppermute | solution.py:21
  254.0 9.6 %collective-permute-start = (bf16[1024,1024]{0,1:T(8,128)(2,1)}, bf16[1024,1024]{0,1:T(8,128)(2,1)}, u32[]{:S(2)}, u32[]{:S(2)}) collective-permute-start(bf16[1024,1024]{0,1:T(8,128)(2,1)} %bitcast.169), channel_id=1, source_target_pairs={{0,4},{4,8},{8,12},{1,5},{5,9},{9,13},{2,6},{6,10},{10,14},{3,7},{... | collective-permute-start | bytes 6291464 | tf_op jit(solution)/shard_map/ppermute | solution.py:20
  267.5 3.1 copy-start.10
  319.3 98.7 %copy-start.1 = (bf16[512,2048]{1,0:T(8,128)(2,1)S(1)}, bf16[512,2048]{1,0:T(8,128)(2,1)}, u32[]{:S(2)}) copy-start(bf16[512,2048]{1,0:T(8,128)(2,1)} %param.15) | copy-start | bytes 6291460
Sparse Core Ops, SparseCore 0:
  57.9 87.3 all-reduce.2
  148.6 85.4 all-reduce.4
  319.4 95.2 reduce-scatter.1
where the time goes:
time: 426 us; the launch traced here: 425 us
  waiting for transfers between devices  249 us (58%)
  matrix products  88.3 us (21%)
  local copies, waits for them, and re-layouts  36.2 us (8%)
  other arithmetic  23 us (5%)
  between operations  13.5 us (3%)
  blocking collectives  8.83 us (2%)
  starting transfers between devices  5.96 us (1%)
    psum x2, waiting for transfers between devices, on_device(): summed = lax.psum(partial, 'head').astype(f32)  153 us
    reduce_scatter x1, waiting for transfers between devices, on_device(): lax.psum_scatter(jnp.dot(attn_two, w_out2, preferred_element_type=f32).as...  95.4 us
    dot_general x1, matrix products, on_device(): jnp.einsum('phts,she->pthe', weights, widened[:, 1], preferred_element_ty...  22.4 us
    unnamed x38, local copies, waits for them, and re-layouts  22.4 us
    dot_general x1, matrix products, on_device(): jnp.einsum('pthe,she->phts', query_tiles, widened[:, 0], preferred_elemen...  19.7 us
    dot_general x2, matrix products, on_device(): proj_n = jnp.dot(normed_n, w_qkv2_flat, preferred_element_type=f32)  12.2 us
    reduce_sum x5, other arithmetic, rms_rows(): mean_sq = jnp.mean(value * value, axis=-1, keepdims=True)  10.8 us
    dot_general x1, matrix products, on_device(): jnp.dot(normed, w_qkv1.reshape(feature_width, 3 * inner_dev), preferred_e...  10.3 us
  transfers between devices with their start and end apart: 5, of which 3 were waited for; matrix products, arithmetic and copies ran while one was open for 6% of the time, Pallas kernels for 0%

commit v1 on v0

--- a/solution.py
+++ b/solution.py
@@ -98,7 +98,7 @@
         if previous is not None:
             partial, previous = lax.optimization_barrier((partial, previous))
             residual_parts[-1] = previous
-        summed = lax.psum(partial, "head").astype(f32)
+        summed = jnp.sum(lax.all_gather(partial, "head"), axis=0).astype(f32)
         tokens_n = tokens[n * block_rows : (n + 1) * block_rows].astype(f32)
         residual_n = (tokens_n + summed).astype(bf16)
         residual_parts.append(residual_n)

time: 426 us -> 565 us (1.33)
  waiting for transfers between devices: 249 us -> 373 us
  other arithmetic: 23 us -> 37.5 us
    all_gather x0 -> x2, waiting for transfers between devices: none -> 278 us  [on_device(): summed = jnp.sum(lax.all_gather(partial, 'head'), axis=0).astype(f32)]
    psum x2 -> x0, waiting for transfers between devices: 153 us -> none  [on_device(): summed = lax.psum(partial, 'head').astype(f32)]
    reduce_sum x0 -> x2, other arithmetic: none -> 14.5 us  [on_device(): summed = jnp.sum(lax.all_gather(partial, 'head'), axis=0).astype(f32)]
  transfers between devices with their start and end apart: 5 -> 5, of which waited for: 3 -> 3; matrix products, arithmetic and copies ran while one was open for 6% -> 4% of each run, Pallas kernels for 0% -> 0%
where the time goes in v1:
time: 565 us; the launch traced here: 564 us
  waiting for transfers between devices  373 us (66%)
  matrix products  88.7 us (16%)
  other arithmetic  37.5 us (7%)
  local copies, waits for them, and re-layouts  36.3 us (6%)
  between operations  13.5 us (2%)
  blocking collectives  8.83 us (2%)
  starting transfers between devices  5.96 us (1%)
    all_gather x2, waiting for transfers between devices, on_device(): summed = jnp.sum(lax.all_gather(partial, 'head'), axis=0).astype(f32)  278 us
    reduce_scatter x1, waiting for transfers between devices, on_device(): lax.psum_scatter(jnp.dot(attn_two, w_out2, preferred_element_type=f32).as...  94.6 us
    unnamed x38, local copies, waits for them, and re-layouts  22.4 us
    dot_general x1, matrix products, on_device(): jnp.einsum('phts,she->pthe', weights, widened[:, 1], preferred_element_ty...  22.4 us
    dot_general x1, matrix products, on_device(): jnp.einsum('pthe,she->phts', query_tiles, widened[:, 0], preferred_elemen...  19.7 us
    reduce_sum x2, other arithmetic, on_device(): summed = jnp.sum(lax.all_gather(partial, 'head'), axis=0).astype(f32)  14.5 us
    dot_general x2, matrix products, on_device(): proj_n = jnp.dot(normed_n, w_qkv2_flat, preferred_element_type=f32)  12.5 us
  transfers between devices with their start and end apart: 5, of which 3 were waited for; matrix products, arithmetic and copies ran while one was open for 4% of the time, Pallas kernels for 0%

profile of v1, /device:TPU:0, one launch (start us, length us, event | category | flops | bytes accessed | tf_op | source)
XLA Modules:
  0.0 563.9 jit_solution(10015666180170650274)
XLA Ops:
  6.5 0.1 iota_compare_fusion
  6.6 3.2 fusion.2
  9.9 8.8 %copy.60 = bf16[2048,3,512]{0,2,1:T(8,128)(2,1)} copy(bf16[2048,3,512]{2,0,1:T(8,128)(2,1)} %param.13) | data formatting | bytes 12582912 | tf_op args[2]
  18.7 10.3 %fusion.12 = f32[1024,3,4,128]{3,0,2,1:T(8,128)S(1)} fusion(bf16[3,4,128,2048]{3,2,1,0:T(8,128)(2,1)} %bitcast.169, bf16[1024,2048]{1,0:T(8,128)(2,1)} %param.11, f32[2048]{0:T(1024)S(1)} %copy-done.15, f32[1024]{0:T(1024)S(1)} %add_rsqrt_fusion.6), kind=kOutput, calls=%fused_computation.21 | convolution fusion | flops 6450839552 | bytes 16789504 | tf_op jit(solution)/shard_map/dot_general | solution.py:56
  29.0 1.1 slice.199
  30.1 1.0 select_convert_fusion.4
  31.1 2.6 fusion.56
  33.7 2.7 fusion.57
  36.4 2.0 fusion.73
  38.5 8.8 %all-gather = bf16[16,128,128]{2,1,0:T(8,128)(2,1)S(1)} all-gather(bf16[4,128,128]{2,1,0:T(8,128)(2,1)S(1)} %get-tuple-element.27), channel_id=2, replica_groups=mesh['groups'=2,'ctx'=4,'head'=4] {'ctx'}, dimensions={0}, use_global_device_ids=true | all-gather | bytes 655360 | tf_op jit(solution)/shard_map/all_gather | solution.py:68
  47.3 0.2 fusion.50
  47.5 0.3 fusion.59
  47.8 0.3 convolution_add_fusion
  48.2 0.4 fusion.58
  48.6 0.4 convolution_add_fusion.1
  48.9 1.1 copy-done.3
  50.0 0.3 copy-done.4
  50.3 0.9 fusion.18
  51.2 0.6 copy-done.2
  51.8 0.9 fusion.17
  52.7 1.1 multiply_reduce_fusion.4
  53.8 1.1 multiply_reduce_fusion.5
  54.9 0.3 multiply_convert_fusion.4
  55.2 2.7 convolution_convert_fusion.1
  57.8 0.0 all-gather.6.cloned.1.call-update
  57.9 0.0 all-gather.8.cloned.1.call-start
  57.9 2.6 convolution_convert_fusion.2
  60.5 148.0 %all-gather.6.cloned.1.call-done = bf16[2048,2048]{1,0:T(8,128)(2,1)} async-done(((bf16[512,2048]{1,0:T(8,128)(2,1)}), bf16[2048,2048]{1,0:T(8,128)(2,1)}) %all-gather.6.cloned.1.call-update) | async-done | bytes 8388624 | tf_op jit(solution)/shard_map/all_gather | solution.py:101
  208.5 7.3 %reduce_sum.137 = bf16[512,2048]{1,0:T(8,128)(2,1)} reduce(bf16[4,512,2048]{2,1,0:T(8,128)(2,1)} %bitcast.166, bf16[]{:T(256)} %constant.40.clone.1), dimensions={0}, to_apply=%region_5.6 | reduce | flops 3145728 | bytes 10485762 | tf_op jit(solution)/shard_map/reduce_sum | solution.py:101
  215.8 3.2 fusion.5
  219.0 0.0 all-gather.8.cloned.1.call-update
  219.0 0.3 reduce-scatter.2.cloned.1.call-start
  219.3 9.5 %copy.71 = bf16[2048,3,512]{0,2,1:T(8,128)(2,1)} copy(bf16[2048,3,512]{2,0,1:T(8,128)(2,1)} %param.17) | data formatting | bytes 12582912 | tf_op args[6]
  228.8 6.0 %fusion.25 = f32[512,3,4,128]{3,0,2,1:T(8,128)S(1)} fusion(bf16[3,4,128,2048]{3,2,1,0:T(8,128)(2,1)} %bitcast.167, bf16[512,2048]{1,0:T(8,128)(2,1)S(1)} %get-tuple-element.7, f32[2048]{0:T(1024)S(1)} %copy-done.16, f32[512]{0:T(512)S(1)} %add_rsqrt_fusion.8), kind=kOutput, calls=%fused_computation.45 | convolution fusion | flops 3225419776 | bytes 11544576 | tf_op jit(solution)/shard_map/dot_general | solution.py:107
  234.8 0.6 multiply_reduce_fusion.3
  235.5 1.0 copy-done.7
  236.4 0.1 fusion.54
  236.5 130.5 %all-gather.8.cloned.1.call-done = bf16[2048,2048]{1,0:T(8,128)(2,1)} async-done(((bf16[512,2048]{1,0:T(8,128)(2,1)}), bf16[2048,2048]{1,0:T(8,128)(2,1)}) %all-gather.8.cloned.1.call-update) | async-done | bytes 8388624 | tf_op jit(solution)/shard_map/all_gather | solution.py:101
  367.0 7.2 %reduce_sum.138 = bf16[512,2048]{1,0:T(8,128)(2,1)} reduce(bf16[4,512,2048]{2,1,0:T(8,128)(2,1)} %bitcast.165, bf16[]{:T(256)} %constant.40.clone.1), dimensions={0}, to_apply=%region_6.7 | reduce | flops 3145728 | bytes 10485762 | tf_op jit(solution)/shard_map/reduce_sum | solution.py:101
  374.2 3.2 fusion.8
  377.5 6.5 %fusion.22 = f32[512,3,4,128]{3,0,2,1:T(8,128)S(1)} fusion(bf16[3,4,128,2048]{3,2,1,0:T(8,128)(2,1)} %bitcast.168, bf16[512,2048]{1,0:T(8,128)(2,1)S(1)} %get-tuple-element.16, f32[512]{0:T(512)S(1)} %add_rsqrt_fusion.7, f32[2048]{0:T(1024)S(1)} %copy-done.16), kind=kOutput, calls=%fused_computation.43 | convolution fusion | flops 3225419776 | bytes 11544576 | tf_op jit(solution)/shard_map/dot_general | solution.py:107
  384.0 0.6 multiply_reduce_fusion.2
  384.6 0.1 fusion.55
  384.7 0.1 maximum_bitcast_fusion.1
  384.8 1.0 copy-done.8
  385.9 1.4 multiply_convert_fusion.2
  387.3 0.1 maximum_bitcast_fusion
  387.4 1.5 pad_maximum_fusion.1
  388.8 4.0 copy.72
  392.8 1.3 collective-permute-start.1
  394.1 4.4 collective-permute-start
  398.5 0.1 and_reduce_fusion
  398.6 0.1 broadcast_bitcast_fusion
  398.7 1.0 pad_maximum_fusion.2
  399.7 3.9 copy.74
  403.7 4.0 copy.73
  407.7 3.1 pad_maximum_fusion
  410.8 19.7 %fusion = (f32[4,4,256]{2,0,1:T(4,128)S(1)}, f32[4,3072,4,256]{3,1,2,0:T(8,128)}) fusion(pred[4,3072]{1,0:T(4,128)(4,1)S(1)} %bitcast.178, bf16[4,256,4,128]{3,1,0,2:T(8,128)(2,1)S(1)} %bitcast.174, bf16[3072,2,4,128]{3,0,2,1:T(8,128)(2,1)S(1)} %pad_maximum_fusion), kind=kOutput, calls=%fused_computation.2 | convolution fusion | flops 3258970112 | bytes 54554624 | tf_op jit(solution)/shard_map/pthe,she->phts/dot_general | solution.py:133
  430.4 22.4 %fusion.40 = bf16[4,256,4,128]{1,3,0,2:T(8,128)(2,1)S(1)} fusion(f32[4,3072,4,256]{3,1,2,0:T(8,128)} %get-tuple-element.34, f32[4,4,256]{2,0,1:T(4,128)S(1)} %get-tuple-element.33, pred[4,3072]{1,0:T(4,128)(4,1)S(1)} %bitcast.179, bf16[3072,2,4,128]{3,0,2,1:T(8,128)(2,1)S(1)} %pad_maximum_fusion), kind=kOutput, calls=%fused_computation.64 | convolution fusion | flops 3272081408 | bytes 54554624 | tf_op jit(solution)/shard_map/phts,she->pthe/dot_general | solution.py:138
  452.8 0.7 copy.77
  453.5 5.9 %convolution_convert_fusion = bf16[1024,2048]{1,0:T(8,128)(2,1)} fusion(bf16[512,2048]{1,0:T(8,128)(2,1)} %param.20, bf16[128,8,4,128]{3,2,1,0:T(4,128)(2,1)S(1)} %bitcast.175), kind=kOutput, calls=%fused_computation.32 | convolution fusion | flops 2149580800 | bytes 7340032 | tf_op jit(solution)/shard_map/dot_general | solution.py:141
  459.4 0.0 reduce-scatter.2.cloned.1.call-update
  459.4 94.6 %reduce-scatter.2.cloned.1.call-done = bf16[256,2048]{1,0:T(8,128)(2,1)} async-done(((bf16[1024,2048]{1,0:T(8,128)(2,1)}), bf16[256,2048]{1,0:T(8,128)(2,1)}) %reduce-scatter.2.cloned.1.call-update) | async-done | bytes 1048592 | tf_op jit(solution)/shard_map/reduce_scatter | solution.py:140
  554.0 3.3 add_convert_fusion.2
  (44 shorter events, 0.2 us)
Async XLA Ops:
  6.5 48.6 %copy-start = (bf16[512,2048]{1,0:T(8,128)(2,1)S(1)}, bf16[512,2048]{1,0:T(8,128)(2,1)}, u32[]{:S(2)}) copy-start(bf16[512,2048]{1,0:T(8,128)(2,1)} %param.15) | copy-start | bytes 6291460
  6.5 202.0 %all-gather.6.cloned.1.call-start = ((), (), s32[]{:S(2)}) async-start(), calls=%async_computation.2 | async-start | bytes 10485760 | tf_op jit(solution)/shard_map/all_gather | solution.py:101
  9.8 8.9 %copy-start.15 = (f32[2048]{0:T(1024)S(1)}, f32[2048]{0:T(1024)}, u32[]{:S(2)}) copy-start(f32[2048]{0:T(1024)} %param.12) | copy-start | bytes 24580
  31.1 2.7 copy-start.9
  47.8 2.2 copy-start.3
  47.8 2.5 copy-start.4
  48.5 3.2 copy-start.2
  53.8 1.1 copy-start.12
  57.9 309.2 %all-gather.8.cloned.1.call-start = ((), (), s32[]{:S(2)}) async-start(), calls=%async_computation.3 | async-start | bytes 10485760 | tf_op jit(solution)/shard_map/all_gather | solution.py:101
  219.0 9.8 %copy-start.5 = (bf16[512,2048]{1,0:T(8,128)(2,1)}, bf16[512,2048]{1,0:T(8,128)(2,1)S(1)}, u32[]{:S(2)}) copy-start(bf16[512,2048]{1,0:T(8,128)(2,1)S(1)} %get-tuple-element.7) | copy-start | bytes 6291460
  219.0 9.8 %copy-start.16 = (f32[2048]{0:T(1024)S(1)}, f32[2048]{0:T(1024)}, u32[]{:S(2)}) copy-start(f32[2048]{0:T(1024)} %param.16) | copy-start | bytes 24580
  219.0 335.0 %reduce-scatter.2.cloned.1.call-start = ((), (), s32[]{:S(2)}) async-start(), calls=%async_computation.1 | async-start | bytes 5242880 | tf_op jit(solution)/shard_map/reduce_scatter | solution.py:140
  234.8 1.6 copy-start.7
  377.4 6.5 %copy-start.6 = (bf16[512,2048]{1,0:T(8,128)(2,1)}, bf16[512,2048]{1,0:T(8,128)(2,1)S(1)}, u32[]{:S(2)}) copy-start(bf16[512,2048]{1,0:T(8,128)(2,1)S(1)} %get-tuple-element.16) | copy-start | bytes 6291460
  384.0 1.9 copy-start.8
  384.0 1.9 copy-start.13
  384.0 1.9 copy-start.14
  387.3 11.1 %copy-start.11 = (s32[4,8]{1,0:T(4,128)S(1)}, s32[4,8]{1,0:T(4,128)}, u32[]{:S(2)}) copy-start(s32[4,8]{1,0:T(4,128)} %param.21) | copy-start | bytes 388
  392.8 6.9 %collective-permute-start.1 = (bf16[1024,1024]{0,1:T(8,128)(2,1)}, bf16[1024,1024]{0,1:T(8,128)(2,1)}, u32[]{:S(2)}, u32[]{:S(2)}) collective-permute-start(bf16[1024,1024]{0,1:T(8,128)(2,1)} %bitcast.172), channel_id=1, source_target_pairs={{4,0},{8,4},{12,8},{5,1},{9,5},{13,9},{6,2},{10,6},{14,10},{7,3},{... | collective-permute-start | bytes 6291464 | tf_op jit(solution)/shard_map/ppermute | solution.py:21
  394.1 9.6 %collective-permute-start = (bf16[1024,1024]{0,1:T(8,128)(2,1)}, bf16[1024,1024]{0,1:T(8,128)(2,1)}, u32[]{:S(2)}, u32[]{:S(2)}) collective-permute-start(bf16[1024,1024]{0,1:T(8,128)(2,1)} %bitcast.173), channel_id=1, source_target_pairs={{0,4},{4,8},{8,12},{1,5},{5,9},{9,13},{2,6},{6,10},{10,14},{3,7},{... | collective-permute-start | bytes 6291464 | tf_op jit(solution)/shard_map/ppermute | solution.py:20
  407.7 3.1 copy-start.10
  459.4 97.9 %copy-start.1 = (bf16[512,2048]{1,0:T(8,128)(2,1)S(1)}, bf16[512,2048]{1,0:T(8,128)(2,1)}, u32[]{:S(2)}) copy-start(bf16[512,2048]{1,0:T(8,128)(2,1)} %param.15) | copy-start | bytes 6291460
Sparse Core Ops, SparseCore 0:
  58.0 150.4 all-gather.5
  219.1 147.8 all-gather.7
  459.5 94.4 reduce-scatter.1
